TPU v7x, 256 devices: a whole 4x4x8 slice. The times are simulated.
256 devices in a mesh: ctx: 8 (over x, core), ch: 32 (over y, z).
Axes of the slice: x: 4, y: 4, z: 8, core: 2. Of those that a mesh axis runs over, the one named last changes fastest.
Arguments:
- tokens_in: bfloat16 [8192, 8192], P(('ctx', 'ch')), may hold values from -6 to 6
- norm_gain: float32 [8192], replicated, may hold values from 0.1 to 1.9
- proj_weight: bfloat16 [3, 8192, 8192], P(None, 'ctx', 'ch'), may hold values from -0.0625 to 0.0625
- conv_weight: float32 [3, 7, 8192], P(None, None, 'ch'), may hold values from -2 to 2
- decay_rate: float32 [16, 8192], P(None, 'ch'), may hold values from 6.1035157e-06 to 0.04
- residue: float32 [16, 8192], P(None, 'ch'), may hold values from -1.5 to 1.5
- skip_gain: float32 [8192], P('ch'), may hold values from -3 to 3
Outputs:
- gated: bfloat16 [8192, 8192], P(('ctx', 'ch'))
All inputs are finite; a program needn't handle non-finite values.
Results may differ from a plain program's by a relative error of at most 0.008.
Values may be sent and summed in bfloat16 or wider, within the bound.
No kernel may reach another device: no remote copies, remote signals or barrier semaphores. Data moves between devices by JAX's collectives and lax.ppermute only.
A program may use at most 128 MiB of HBM per device.

v0:
```python
import jax
import jax.numpy as jnp
from jax import lax
from jax.sharding import PartitionSpec as P

norm_eps = 1e-05


def shifted(shard, axis, by):
    length = lax.axis_size(axis)
    pairs = [(i, i + by) for i in range(length) if 0 <= i + by < length]
    return lax.ppermute(shard, axis, pairs)


def on_device(tokens_in, norm_gain, proj_weight, conv_weight, decay_rate, residue, skip_gain):
    widened = tokens_in.astype(jnp.float32)
    mean_square = jnp.mean(widened * widened, axis=-1, keepdims=True)
    normed = (widened * lax.rsqrt(mean_square + norm_eps) * norm_gain[None, :]).astype(jnp.bfloat16)
    gathered = lax.all_gather(normed, "ch", axis=0, tiled=True)
    row_count = gathered.shape[0]
    chan_count = proj_weight.shape[2]
    summed = jnp.einsum(
        "tf,ifc->itc",
        gathered,
        lax.all_gather(proj_weight, "ctx", axis=1, tiled=True),
        preferred_element_type=jnp.float32,
    )
    projected = summed.astype(jnp.bfloat16)
    tap_count = conv_weight.shape[1]
    reach = tap_count - 1
    rim_rows = shifted(projected[:, row_count - reach :, :], "ctx", 1)
    padded = jnp.concatenate([rim_rows, projected], axis=1).astype(jnp.float32)
    featured = jnp.zeros((3, row_count, chan_count), jnp.float32)
    for shift_idx in range(tap_count):
        featured = (
            featured
            + conv_weight[:, shift_idx, None, :]
            * padded[:, reach - shift_idx : reach - shift_idx + row_count, :]
        )
    queries = featured[0]
    mixed = featured[1] * featured[2]
    highest = lax.Precision.HIGHEST
    in_scale = jnp.sqrt(-jnp.expm1(-2.0 * decay_rate))
    span_rows = min(128, row_count)
    span_count = row_count // span_rows
    positions = jnp.arange(span_rows, dtype=jnp.float32)
    lag_decay = jnp.exp(-decay_rate[:, None, :] * positions[None, :, None])
    impulse = jnp.sum((residue * in_scale)[:, None, :] * lag_decay, axis=0)
    offsets = jnp.arange(span_rows)[:, None] - jnp.arange(span_rows)[None, :]
    lag_table = (offsets[None, :, :] == jnp.arange(span_rows)[:, None, None]).astype(jnp.float32)
    toeplitz = jnp.einsum("lc,lts->cts", impulse, lag_table, precision=highest)
    spans_in = mixed.reshape(span_count, span_rows, chan_count)
    inside = jnp.einsum("cts,jsc->jtc", toeplitz, spans_in, precision=highest)
    end_weight = in_scale[:, None, :] * jnp.exp(
        -decay_rate[:, None, :] * (span_rows - 1.0 - positions)[None, :, None]
    )
    span_ends = jnp.einsum("jsc,msc->jmc", spans_in, end_weight, precision=highest)
    span_decay = jnp.exp(-decay_rate * float(span_rows))

    def advance(carried, span_end):
        return (span_decay * carried + span_end, carried)

    zero_state = jnp.zeros(decay_rate.shape, jnp.float32)
    local_end, starts = lax.scan(advance, zero_state, span_ends)
    whole_decay = jnp.exp(-decay_rate * float(row_count))

    def handoff(unused_turn, incoming):
        return shifted(whole_decay * incoming + local_end, "ctx", 1)

    incoming = lax.fori_loop(0, lax.axis_size("ctx") - 1, handoff, zero_state)
    span_starts = jnp.arange(span_count, dtype=jnp.float32) * float(span_rows)
    starts = (
        starts
        + jnp.exp(-decay_rate[None, :, :] * span_starts[:, None, None]) * incoming[None, :, :]
    )
    out_weight = residue[:, None, :] * jnp.exp(
        -decay_rate[:, None, :] * (positions + 1.0)[None, :, None]
    )
    outside = jnp.einsum("jmc,mtc->jtc", starts, out_weight, precision=highest)
    filtered = (inside + outside).reshape(row_count, chan_count)
    gated = (queries * (filtered + skip_gain[None, :] * mixed)).astype(jnp.bfloat16)
    return lax.all_to_all(gated, "ch", split_axis=0, concat_axis=1, tiled=True)


def solution(mesh):
    in_specs = (
        P(("ctx", "ch"), None),
        P(),
        P(None, "ctx", "ch"),
        P(None, None, "ch"),
        P(None, "ch"),
        P(None, "ch"),
        P("ch"),
    )
    out_specs = P(("ctx", "ch"), None)
    return jax.shard_map(
        on_device, mesh=mesh, in_specs=in_specs, out_specs=out_specs, check_vma=False
    )
```

profile of v0, /device:TPU:34, one launch (start us, length us, event | category | flops | bytes accessed | tf_op | source)
XLA Modules:
  0.0 376.8 jit_solution(1986812862186608656)
XLA Ops:
  6.5 0.7 all-gather.5.cloned.1.call-update
  7.3 1.3 fusion.38
  8.6 2.0 fusion.40
  10.9 1.7 multiply_reduce_fusion
  12.7 9.6 %fusion.4 = f32[256,128,128]{2,0,1:T(8,128)} fusion(s32[128,128]{1,0:T(8,128)S(1)} %iota_subtract_fusion, f32[128,256]{0,1:T(8,128)S(1)} %multiply_reduce_fusion), kind=kOutput, calls=%fused_computation.8 | convolution fusion | flops 6444548096 | bytes 16973824 | tf_op jit(solution)/shard_map/lc,lts->cts/dot_general | solution.py:51
  22.2 58.8 %all-gather.5.cloned.1.call-done = bf16[3,8192,256]{2,1,0:T(8,128)(2,1)} async-done(((bf16[3,1024,256]{2,1,0:T(8,128)(2,1)}), bf16[3,8192,256]{2,1,0:T(8,128)(2,1)}) %all-gather.5.cloned.1.call-update) | async-done | bytes 12582928 | tf_op jit(solution)/shard_map/all_gather | solution.py:25
  81.0 141.5 %all-gather.3.cloned.1.call-done = bf16[1024,8192]{1,0:T(8,128)(2,1)} async-done(((bf16[32,8192]{1,0:T(8,128)(2,1)}), bf16[1024,8192]{1,0:T(8,128)(2,1)}) %all-gather.3.cloned.1.call-update) | async-done | bytes 16777232 | tf_op jit(solution)/shard_map/all_gather | solution.py:19
  222.6 18.7 %fusion.23 = bf16[3,1024,256]{2,1,0:T(8,128)(2,1)S(1)} fusion(bf16[3,8192,256]{2,1,0:T(8,128)(2,1)} %all-gather.5.cloned.1.call-done, bf16[1024,8192]{1,0:T(8,128)(2,1)} %all-gather.3.cloned.1.call-done), kind=kOutput, calls=%fused_computation.34 | convolution fusion | flops 12885688320 | bytes 30932992 | tf_op jit(solution)/shard_map/tf,ifc->itc/dot_general | solution.py:22
  241.3 2.1 collective-permute-start.1
  243.4 0.7 copy.31
  244.3 2.0 collective-permute-done.1
  246.3 0.3 maximum_convert_fusion
  246.6 2.6 fusion.6
  249.4 0.4 copy.29
  249.8 38.4 %fusion.32 = f32[8,128,256]{1,0,2:T(8,128)} fusion(f32[8,128,256]{1,0,2:T(8,128)S(1)} %copy.29, f32[256,128,128]{2,0,1:T(8,128)} %fusion.4), kind=kOutput, calls=%fused_computation.37 | convolution fusion | flops 402653184 | bytes 18874368 | tf_op jit(solution)/shard_map/cts,jsc->jtc/dot_general | solution.py:53
  288.2 5.2 %fusion.29 = f32[8,16,256]{1,0,2:T(8,128)} fusion(f32[8,128,256]{1,0,2:T(8,128)S(1)} %copy.29, f32[128]{0:T(128)S(1)} %iota_subtract_fusion.1, f32[16,256]{0,1:T(8,128)S(1)} %copy.32, f32[16,256]{0,1:T(8,128)S(1)} %copy.28), kind=kOutput, calls=%fused_computation.36 | convolution fusion | flops 51380224 | bytes 1212928 | tf_op jit(solution)/shard_map/jsc,msc->jmc/dot_general | solution.py:57
  293.4 1.6 copy.34
  295.0 4.9 %while.24 = (s32[]{:T(128)}, f32[16,256]{1,0:T(8,128)S(1)}, f32[8,16,256]{2,1,0:T(8,128)}, f32[16,256]{1,0:T(8,128)S(1)}, f32[8,16,256]{2,1,0:T(8,128)S(1)}, /*index=5*/s32[]{:T(128)}, s32[]{:T(128)}) while((s32[]{:T(128)}, f32[16,256]{1,0:T(8,128)S(1)}, f32[8,16,256]{2,1,0:T(8,128)}, f32[16,256]{1,0:T(8,128)S(1)}, ...), condition=%wide.region_3.4_spmd.clone, body=%wide.region_2.3_spmd.clone.sunk | while | flops 16387 | bytes 98408 | solution.py:64
  295.0 0.6 bitcast_dynamic-update-slice_fusion.2
  295.6 0.6 bitcast_dynamic-update-slice_fusion.2
  296.2 0.6 bitcast_dynamic-update-slice_fusion.2
  296.8 0.6 bitcast_dynamic-update-slice_fusion.2
  297.4 0.6 bitcast_dynamic-update-slice_fusion.2
  298.1 0.6 bitcast_dynamic-update-slice_fusion.2
  298.7 0.6 bitcast_dynamic-update-slice_fusion.2
  299.3 0.6 bitcast_dynamic-update-slice_fusion.2
  299.9 35.4 %while.23 = (s32[]{:T(128)}, f32[16,256]{1,0:T(8,128)S(1)}, f32[16,256]{1,0:T(8,128)S(1)}, f32[16,256]{1,0:T(8,128)S(1)}, s32[]{:T(128)}) while((s32[]{:T(128)}, f32[16,256]{1,0:T(8,128)S(1)}, f32[16,256]{1,0:T(8,128)S(1)}, f32[16,256]{1,0:T(8,128)S(1)}, s32[]{:T(128)}) %tuple.55), condition=%wide.region_5.6_spmd, body=%wide.region_4.5_spmd.sunk | while | flops 8194 | bytes 131173 | solution.py:70
  299.9 1.9 collective-permute-start
  301.9 3.1 collective-permute-done
  305.0 1.9 collective-permute-start
  306.9 3.1 collective-permute-done
  310.1 1.9 collective-permute-start
  312.0 3.1 collective-permute-done
  315.1 1.9 collective-permute-start
  317.0 3.1 collective-permute-done
  320.2 1.9 collective-permute-start
  322.1 3.1 collective-permute-done
  325.2 1.9 collective-permute-start
  327.1 3.1 collective-permute-done
  330.3 1.9 collective-permute-start
  332.2 3.1 collective-permute-done
  335.3 1.0 multiply_add_fusion.1
  336.3 1.3 copy.35
  337.7 5.0 %fusion.35 = f32[8,128,256]{1,0,2:T(8,128)} fusion(f32[8,128,256]{1,0,2:T(8,128)S(1)} %copy-done, f32[8,16,256]{1,0,2:T(8,128)} %copy.35, f32[128]{0:T(128)S(1)} %iota_add_fusion, f32[16,256]{0,1:T(8,128)} %copy.31, f32[16,256]{0,1:T(8,128)S(1)} %copy.28), kind=kOutput, calls=%fused_computation.38 | convolution fusion | flops 51642368 | bytes 2261504 | tf_op jit(solution)/shard_map/jmc,mtc->jtc/dot_general | solution.py:79
  342.6 1.6 copy.36
  344.2 0.4 multiply_convert_fusion
  344.6 24.5 %all_to_all.16 = bf16[32,32,256]{2,1,0:T(8,128)(2,1)S(1)} all-to-all(bf16[32,32,256]{2,1,0:T(8,128)(2,1)S(1)} %multiply_convert_fusion), channel_id=1, replica_groups=mesh['ctx'=8,'ch'=32] {'ch'}, dimensions={0} | all-to-all | bytes 1048576 | tf_op jit(solution)/shard_map/all_to_all | solution.py:82
  369.1 0.8 copy.45
  (47 shorter events, 0.8 us)
Async XLA Ops:
  6.5 4.1 %copy-start.3 = (f32[16,256]{1,0:T(8,128)S(1)}, f32[16,256]{1,0:T(8,128)}, u32[]{:S(2)}) copy-start(f32[16,256]{1,0:T(8,128)} %param.15) | copy-start | bytes 49156
  6.5 4.1 %copy-start.1 = (f32[16,256]{1,0:T(8,128)S(1)}, f32[16,256]{1,0:T(8,128)}, u32[]{:S(2)}) copy-start(f32[16,256]{1,0:T(8,128)} %param.16) | copy-start | bytes 49156
  6.5 6.1 %copy-start.2 = (f32[3,7,256]{2,1,0:T(8,128)S(1)}, f32[3,7,256]{2,1,0:T(8,128)}, u32[]{:S(2)}) copy-start(f32[3,7,256]{2,1,0:T(8,128)} %param.14) | copy-start | bytes 64516
  6.5 74.5 %all-gather.5.cloned.1.call-start = ((), (), s32[]{:S(2)}) async-start(), calls=%async_computation.2 | async-start | bytes 14155776 | tf_op jit(solution)/shard_map/all_gather | solution.py:25
  7.3 215.3 %all-gather.3.cloned.1.call-start = ((), (), s32[]{:S(2)}) async-start(), calls=%async_computation.1 | async-start | bytes 17301504 | tf_op jit(solution)/shard_map/all_gather | solution.py:19
  241.3 5.0 %collective-permute-start.1 = (bf16[3,6,256]{2,1,0:T(8,128)(2,1)S(1)}, bf16[3,6,256]{2,1,0:T(8,128)(2,1)S(1)}, u32[]{:S(2)}, u32[]{:S(2)}) collective-permute-start(bf16[3,6,256]{2,1,0:T(8,128)(2,1)S(1)} %slice.72), channel_id=1, source_target_pairs={{0,32},{32,64},{64,96},{96,128},{128,160},{160,192},{192,224},{1,3... | collective-permute-start | bytes 27656 | tf_op jit(solution)/shard_map/ppermute | solution.py:12
  293.4 44.3 %copy-start = (f32[8,128,256]{1,0,2:T(8,128)S(1)}, f32[8,128,256]{1,0,2:T(8,128)}, u32[]{:S(2)}) copy-start(f32[8,128,256]{1,0,2:T(8,128)} %fusion.32) | copy-start | bytes 3145732
  299.9 5.1 %collective-permute-start = (f32[16,256]{1,0:T(8,128)S(1)}, f32[16,256]{1,0:T(8,128)S(1)}, u32[]{:S(2)}, u32[]{:S(2)}) collective-permute-start(f32[16,256]{1,0:T(8,128)S(1)} %multiply_add_fusion.3), channel_id=1, source_target_pairs={{0,32},{32,64},{64,96},{96,128},{128,160},{160,192},{192,224},{1,3... | collective-permute-start | bytes 49160 | tf_op jit(solution)/shard_map/while/body/eval_jaxpr/ppermute | solution.py:12
  305.0 5.0 %collective-permute-start = (f32[16,256]{1,0:T(8,128)S(1)}, f32[16,256]{1,0:T(8,128)S(1)}, u32[]{:S(2)}, u32[]{:S(2)}) collective-permute-start(f32[16,256]{1,0:T(8,128)S(1)} %multiply_add_fusion.3), channel_id=1, source_target_pairs={{0,32},{32,64},{64,96},{96,128},{128,160},{160,192},{192,224},{1,3... | collective-permute-start | bytes 49160 | tf_op jit(solution)/shard_map/while/body/eval_jaxpr/ppermute | solution.py:12
  310.1 5.0 %collective-permute-start = (f32[16,256]{1,0:T(8,128)S(1)}, f32[16,256]{1,0:T(8,128)S(1)}, u32[]{:S(2)}, u32[]{:S(2)}) collective-permute-start(f32[16,256]{1,0:T(8,128)S(1)} %multiply_add_fusion.3), channel_id=1, source_target_pairs={{0,32},{32,64},{64,96},{96,128},{128,160},{160,192},{192,224},{1,3... | collective-permute-start | bytes 49160 | tf_op jit(solution)/shard_map/while/body/eval_jaxpr/ppermute | solution.py:12
  315.1 5.0 %collective-permute-start = (f32[16,256]{1,0:T(8,128)S(1)}, f32[16,256]{1,0:T(8,128)S(1)}, u32[]{:S(2)}, u32[]{:S(2)}) collective-permute-start(f32[16,256]{1,0:T(8,128)S(1)} %multiply_add_fusion.3), channel_id=1, source_target_pairs={{0,32},{32,64},{64,96},{96,128},{128,160},{160,192},{192,224},{1,3... | collective-permute-start | bytes 49160 | tf_op jit(solution)/shard_map/while/body/eval_jaxpr/ppermute | solution.py:12
  320.2 5.0 %collective-permute-start = (f32[16,256]{1,0:T(8,128)S(1)}, f32[16,256]{1,0:T(8,128)S(1)}, u32[]{:S(2)}, u32[]{:S(2)}) collective-permute-start(f32[16,256]{1,0:T(8,128)S(1)} %multiply_add_fusion.3), channel_id=1, source_target_pairs={{0,32},{32,64},{64,96},{96,128},{128,160},{160,192},{192,224},{1,3... | collective-permute-start | bytes 49160 | tf_op jit(solution)/shard_map/while/body/eval_jaxpr/ppermute | solution.py:12
  325.2 5.0 %collective-permute-start = (f32[16,256]{1,0:T(8,128)S(1)}, f32[16,256]{1,0:T(8,128)S(1)}, u32[]{:S(2)}, u32[]{:S(2)}) collective-permute-start(f32[16,256]{1,0:T(8,128)S(1)} %multiply_add_fusion.3), channel_id=1, source_target_pairs={{0,32},{32,64},{64,96},{96,128},{128,160},{160,192},{192,224},{1,3... | collective-permute-start | bytes 49160 | tf_op jit(solution)/shard_map/while/body/eval_jaxpr/ppermute | solution.py:12
  330.3 5.0 %collective-permute-start = (f32[16,256]{1,0:T(8,128)S(1)}, f32[16,256]{1,0:T(8,128)S(1)}, u32[]{:S(2)}, u32[]{:S(2)}) collective-permute-start(f32[16,256]{1,0:T(8,128)S(1)} %multiply_add_fusion.3), channel_id=1, source_target_pairs={{0,32},{32,64},{64,96},{96,128},{128,160},{160,192},{192,224},{1,3... | collective-permute-start | bytes 49160 | tf_op jit(solution)/shard_map/while/body/eval_jaxpr/ppermute | solution.py:12
  337.7 6.5 %copy-start.4 = (f32[256]{0:T(256)S(1)}, f32[256]{0:T(256)}, u32[]{:S(2)}) copy-start(f32[256]{0:T(256)} %param.17) | copy-start | bytes 3076
Sparse Core Ops, SparseCore 0:
  9.2 71.7 all-gather.4
  83.6 138.9 all-gather.2
where the time goes:
time: 377 us
  waiting for transfers between devices  225 us (60%)
  matrix products  76.7 us (20%)
  blocking collectives  24.5 us (6%)
  starting transfers between devices  15.5 us (4%)
  other arithmetic  14.5 us (4%)
  between operations  13.6 us (4%)
  local copies, waits for them, and re-layouts  6.84 us (2%)
    all_gather x1, waiting for transfers between devices, on_device(): gathered = lax.all_gather(normed, 'ch', axis=0, tiled=True)  142 us
    all_gather x1, waiting for transfers between devices, on_device(): lax.all_gather(proj_weight, 'ctx', axis=1, tiled=True)  58.8 us
    dot_general x1, matrix products, on_device(): inside = jnp.einsum('cts,jsc->jtc', toeplitz, spans_in, precision=highest)  38.4 us
    all_to_all x1, blocking collectives, on_device(): return lax.all_to_all(gated, 'ch', split_axis=0, concat_axis=1, tiled=True)  24.5 us
    ppermute x8, waiting for transfers between devices, shifted(): return lax.ppermute(shard, axis, pairs)  23.9 us
    dot_general x1, matrix products, on_device(): jnp.einsum('tf,ifc->itc', gathered, lax.all_gather(proj_weight, 'ctx', ax...  18.7 us
    ppermute x8, starting transfers between devices, shifted(): return lax.ppermute(shard, axis, pairs)  15.5 us
    dot_general x1, matrix products, on_device(): toeplitz = jnp.einsum('lc,lts->cts', impulse, lag_table, precision=highest)  9.55 us
  transfers between devices with their start and end apart: 10, of which 10 were waited for; matrix products, arithmetic and copies ran while one was open for 4% of the time, Pallas kernels for 0%

commit v1 on v0

--- a/solution.py
+++ b/solution.py
@@ -16,7 +16,9 @@
     widened = tokens_in.astype(jnp.float32)
     mean_square = jnp.mean(widened * widened, axis=-1, keepdims=True)
     normed = (widened * lax.rsqrt(mean_square + norm_eps) * norm_gain[None, :]).astype(jnp.bfloat16)
-    gathered = lax.all_gather(normed, "ch", axis=0, tiled=True)
+    gathered = jnp.concatenate(
+        lax.all_to_all(jnp.stack([normed] * lax.axis_size("ch")), "ch", 0, 0), axis=0
+    )
     row_count = gathered.shape[0]
     chan_count = proj_weight.shape[2]
     summed = jnp.einsum(

time: 377 us -> 593 us (1.57)
  waiting for transfers between devices: 225 us -> 402 us
  blocking collectives: 24.5 us -> 46.9 us
  starting transfers between devices: 15.5 us -> 27.1 us
  local copies, waits for them, and re-layouts: 6.84 us -> 12.8 us
    all_to_all x0 -> x1, waiting for transfers between devices: none -> 317 us  [on_device(): lax.all_to_all(jnp.stack([normed] * lax.axis_size('ch')), 'ch', 0, 0)]
    all_gather x1 -> x0, waiting for transfers between devices: 142 us -> none  [on_device(): gathered = lax.all_gather(normed, 'ch', axis=0, tiled=True)]
    all_to_all x1, blocking collectives: 24.5 us -> 46.9 us  [on_device(): return lax.all_to_all(gated, 'ch', split_axis=0, concat_axis=1, tiled=True)]
    all_to_all x0 -> x1, starting transfers between devices: none -> 11.5 us  [on_device(): lax.all_to_all(jnp.stack([normed] * lax.axis_size('ch')), 'ch', 0, 0)]
    another operation x0 -> x1, local copies, waits for them, and re-layouts: none -> 5.99 us  [on_device(): jnp.stack([normed] * lax.axis_size('ch'))]
  transfers between devices with their start and end apart: 10 -> 10, of which waited for: 10 -> 10; matrix products, arithmetic and copies ran while one was open for 4% -> 2% of each run, Pallas kernels for 0% -> 0%
where the time goes in v1:
time: 593 us
  waiting for transfers between devices  402 us (68%)
  matrix products  76.7 us (13%)
  blocking collectives  46.9 us (8%)
  starting transfers between devices  27.1 us (5%)
  other arithmetic  13.7 us (2%)
  between operations  13.6 us (2%)
  local copies, waits for them, and re-layouts  12.8 us (2%)
    all_to_all x1, waiting for transfers between devices, on_device(): lax.all_to_all(jnp.stack([normed] * lax.axis_size('ch')), 'ch', 0, 0)  317 us
    all_gather x1, waiting for transfers between devices, on_device(): lax.all_gather(proj_weight, 'ctx', axis=1, tiled=True)  60.6 us
    all_to_all x1, blocking collectives, on_device(): return lax.all_to_all(gated, 'ch', split_axis=0, concat_axis=1, tiled=True)  46.9 us
    dot_general x1, matrix products, on_device(): inside = jnp.einsum('cts,jsc->jtc', toeplitz, spans_in, precision=highest)  38.4 us
    ppermute x8, waiting for transfers between devices, shifted(): return lax.ppermute(shard, axis, pairs)  23.9 us
    dot_general x1, matrix products, on_device(): jnp.einsum('tf,ifc->itc', gathered, lax.all_gather(proj_weight, 'ctx', ax...  18.7 us
    ppermute x8, starting transfers between devices, shifted(): return lax.ppermute(shard, axis, pairs)  15.5 us
  transfers between devices with their start and end apart: 10, of which 10 were waited for; matrix products, arithmetic and copies ran while one was open for 2% of the time, Pallas kernels for 0%

profile of v1, /device:TPU:34, one launch (start us, length us, event | category | flops | bytes accessed | tf_op | source)
XLA Modules:
  0.0 592.7 jit_solution(4145409154433120103)
XLA Ops:
  6.5 1.2 fusion.31
  7.8 1.2 fusion.33
  9.0 6.0 %stack.2 = bf16[32,32,8192]{2,1,0:T(8,128)(2,1)} broadcast(bf16[32,8192]{1,0:T(8,128)(2,1)S(1)} %fusion.33), dimensions={1,2} | broadcast | bytes 17301504 | tf_op jit(solution)/shard_map/stack | solution.py:20
  15.0 11.5 %all-to-all-start = ((bf16[32,32,8192]{2,1,0:T(8,128)(2,1)}), bf16[32,32,8192]{2,1,0:T(8,128)(2,1)}, u32[]{:S(2)}, u32[]{:S(2)}) async-start(bf16[32,32,8192]{2,1,0:T(8,128)(2,1)} %stack.2), calls=%async_computation | async-start | bytes 33554432 | tf_op jit(solution)/shard_map/all_to_all | solution.py:20
  26.6 0.7 all-gather.2.cloned.1.call-update
  27.6 1.7 multiply_reduce_fusion
  29.4 9.6 %fusion.2 = f32[256,128,128]{2,0,1:T(8,128)} fusion(s32[128,128]{1,0:T(8,128)S(1)} %iota_subtract_fusion, f32[128,256]{0,1:T(8,128)S(1)} %multiply_reduce_fusion), kind=kOutput, calls=%fused_computation.6 | convolution fusion | flops 6444548096 | bytes 16973824 | tf_op jit(solution)/shard_map/lc,lts->cts/dot_general | solution.py:53
  38.9 60.6 %all-gather.2.cloned.1.call-done = bf16[3,8192,256]{2,1,0:T(8,128)(2,1)} async-done(((bf16[3,1024,256]{2,1,0:T(8,128)(2,1)}), bf16[3,8192,256]{2,1,0:T(8,128)(2,1)}) %all-gather.2.cloned.1.call-update) | async-done | bytes 12582928 | tf_op jit(solution)/shard_map/all_gather | solution.py:27
  99.5 316.6 %all-to-all-done = bf16[32,32,8192]{2,1,0:T(8,128)(2,1)} async-done(((bf16[32,32,8192]{2,1,0:T(8,128)(2,1)}), bf16[32,32,8192]{2,1,0:T(8,128)(2,1)}, u32[]{:S(2)}, u32[]{:S(2)}) %all-to-all-start) | async-done | bytes 16777248 | tf_op jit(solution)/shard_map/all_to_all | solution.py:20
  416.1 18.7 %fusion.18 = bf16[3,1024,256]{2,1,0:T(8,128)(2,1)S(1)} fusion(bf16[1024,8192,1]{1,0,2:T(8,128)(2,1)} %bitcast.1, bf16[3,8192,256]{2,1,0:T(8,128)(2,1)} %all-gather.2.cloned.1.call-done), kind=kOutput, calls=%fused_computation.32 | convolution fusion | flops 12885688320 | bytes 30932992 | tf_op jit(solution)/shard_map/tf,ifc->itc/dot_general | solution.py:24
  434.9 2.1 collective-permute-start.1
  437.0 0.8 copy.31
  437.9 2.0 collective-permute-done.1
  440.2 2.6 fusion.4
  443.0 0.4 copy.29
  443.4 38.4 %fusion.25 = f32[8,128,256]{1,0,2:T(8,128)} fusion(f32[8,128,256]{1,0,2:T(8,128)S(1)} %copy.29, f32[256,128,128]{2,0,1:T(8,128)} %fusion.2), kind=kOutput, calls=%fused_computation.35 | convolution fusion | flops 402653184 | bytes 18874368 | tf_op jit(solution)/shard_map/cts,jsc->jtc/dot_general | solution.py:55
  481.8 5.2 fusion.22
  486.9 1.6 copy.34
  488.6 4.9 while.24
  488.6 0.6 bitcast_dynamic-update-slice_fusion.2
  489.2 0.6 bitcast_dynamic-update-slice_fusion.2
  489.8 0.6 bitcast_dynamic-update-slice_fusion.2
  490.4 0.6 bitcast_dynamic-update-slice_fusion.2
  491.0 0.6 bitcast_dynamic-update-slice_fusion.2
  491.6 0.6 bitcast_dynamic-update-slice_fusion.2
  492.3 0.6 bitcast_dynamic-update-slice_fusion.2
  492.9 0.6 bitcast_dynamic-update-slice_fusion.2
  493.5 35.4 %while.23 = (s32[]{:T(128)}, f32[16,256]{1,0:T(8,128)S(1)}, f32[16,256]{1,0:T(8,128)S(1)}, f32[16,256]{1,0:T(8,128)S(1)}, s32[]{:T(128)}) while((s32[]{:T(128)}, f32[16,256]{1,0:T(8,128)S(1)}, f32[16,256]{1,0:T(8,128)S(1)}, f32[16,256]{1,0:T(8,128)S(1)}, s32[]{:T(128)}) %tuple.55), condition=%wide.region_5.6_spmd, body=%wide.region_4.5_spmd.sunk | while | flops 8194 | bytes 131173 | solution.py:72
  493.5 1.9 collective-permute-start
  495.5 3.1 collective-permute-done
  498.6 1.9 collective-permute-start
  500.5 3.1 collective-permute-done
  503.7 1.9 collective-permute-start
  505.6 3.1 collective-permute-done
  508.7 1.9 collective-permute-start
  510.6 3.1 collective-permute-done
  513.8 1.9 collective-permute-start
  515.7 3.1 collective-permute-done
  518.8 1.9 collective-permute-start
  520.7 3.1 collective-permute-done
  523.9 1.9 collective-permute-start
  525.8 3.1 collective-permute-done
  528.9 1.0 multiply_add_fusion.1
  529.9 1.3 copy.35
  531.2 5.0 fusion.28
  536.2 1.6 copy.36
  538.1 46.9 %all_to_all.21 = bf16[32,32,256]{2,1,0:T(8,128)(2,1)S(1)} all-to-all(bf16[32,32,256]{2,1,0:T(8,128)(2,1)S(1)} %multiply_convert_fusion), channel_id=1, replica_groups=mesh['ctx'=8,'ch'=32] {'ch'}, dimensions={0} | all-to-all | bytes 1048576 | tf_op jit(solution)/shard_map/all_to_all | solution.py:84
  585.0 0.8 copy.45
  (47 shorter events, 1.4 us)
Async XLA Ops:
  15.0 12.3 %copy-start.1 = (f32[16,256]{1,0:T(8,128)S(1)}, f32[16,256]{1,0:T(8,128)}, u32[]{:S(2)}) copy-start(f32[16,256]{1,0:T(8,128)} %param.16) | copy-start | bytes 49156
  15.0 12.3 %copy-start.3 = (f32[16,256]{1,0:T(8,128)S(1)}, f32[16,256]{1,0:T(8,128)}, u32[]{:S(2)}) copy-start(f32[16,256]{1,0:T(8,128)} %param.15) | copy-start | bytes 49156
  15.0 14.3 %copy-start.2 = (f32[3,7,256]{2,1,0:T(8,128)S(1)}, f32[3,7,256]{2,1,0:T(8,128)}, u32[]{:S(2)}) copy-start(f32[3,7,256]{2,1,0:T(8,128)} %param.14) | copy-start | bytes 64516
  15.0 401.1 %all-to-all-start = ((bf16[32,32,8192]{2,1,0:T(8,128)(2,1)}), bf16[32,32,8192]{2,1,0:T(8,128)(2,1)}, u32[]{:S(2)}, u32[]{:S(2)}) async-start(bf16[32,32,8192]{2,1,0:T(8,128)(2,1)} %stack.2), calls=%async_computation | async-start | bytes 33554432 | tf_op jit(solution)/shard_map/all_to_all | solution.py:20
  26.6 72.9 %all-gather.2.cloned.1.call-start = ((), (), s32[]{:S(2)}) async-start(), calls=%async_computation.2 | async-start | bytes 14155776 | tf_op jit(solution)/shard_map/all_gather | solution.py:27
  434.9 5.0 collective-permute-start.1
  486.9 44.3 %copy-start = (f32[8,128,256]{1,0,2:T(8,128)S(1)}, f32[8,128,256]{1,0,2:T(8,128)}, u32[]{:S(2)}) copy-start(f32[8,128,256]{1,0,2:T(8,128)} %fusion.25) | copy-start | bytes 3145732
  493.5 5.1 collective-permute-start
  498.6 5.0 collective-permute-start
  503.7 5.0 collective-permute-start
  508.7 5.0 collective-permute-start
  513.8 5.0 collective-permute-start
  518.8 5.0 collective-permute-start
  523.9 5.0 collective-permute-start
  531.2 6.5 %copy-start.4 = (f32[256]{0:T(256)S(1)}, f32[256]{0:T(256)}, u32[]{:S(2)}) copy-start(f32[256]{0:T(256)} %param.17) | copy-start | bytes 3076
Sparse Core Ops, SparseCore 0:
  29.2 70.2 all-gather.1
